TPU v7x, 32 devices: a whole 2x2x4 slice. The times are simulated.
32 devices in a mesh: blk: 8 (over z, core), vb: 4 (over y, x).
Axes of the slice: x: 2, y: 2, z: 4, core: 2. Of those that a mesh axis runs over, the one named last changes fastest.
Arguments:
- amplitudes: float32 [32, 1024, 1024], P('blk', 'vb'), may hold values from -6 to 6
- integrals: float32 [2048, 1024], P('blk'), may hold values from -0.5 to 0.5
- row_orbitals: int32 [2048], P('blk'), may hold values from 0 to 1023
- pair_orbitals: int32 [32, 2], P('blk'), may hold values from 0 to 255
- occupied_energy: float32 [256], replicated, may hold values from -2 to -0.5
- virtual_energy: float32 [1024], replicated, may hold values from 0.5 to 3
Outputs:
- density: float32 [32, 1024, 1024], P('blk', 'vb')
All inputs are finite; a program needn't handle non-finite values.
Results may differ from a plain program's by a relative error of at most 0.0003.
Values sent between devices are 32-bit elements; how exact they have to be, the bound alone decides.
No kernel may reach another device: no remote copies, remote signals or barrier semaphores. Data moves between devices by JAX's collectives and lax.ppermute only.
A program may use at most 64 MiB of HBM per device.

v0:
```python
import jax
import jax.numpy as jnp
from jax import lax
from jax.sharding import PartitionSpec as P

HOPS = 5


def passed_along(block, axis, distance):
    devices = range(lax.axis_size(axis))
    route = [((i - distance) % len(devices), i) for i in devices]
    return lax.ppermute(block, axis, route)


def step_down(carried):
    return passed_along(carried, "blk", 1)


def local(amplitudes, integrals, row_orbitals, pair_orbitals, occupied_energy, virtual_energy):
    width = virtual_energy.shape[0]
    nocc = occupied_energy.shape[0]
    quarter = width // lax.axis_size("vb")
    qstart = lax.axis_index("vb") * quarter
    virt_iota = jnp.arange(width, dtype=jnp.int32)
    occ_iota = jnp.arange(nocc, dtype=jnp.int32)
    row_energy = jnp.sum(
        jnp.where(row_orbitals[:, None] == virt_iota[None, :], virtual_energy[None, :], 0.0), axis=1
    )
    pair_match = pair_orbitals[:, :, None] == occ_iota[None, None, :]
    pair_energy = jnp.sum(jnp.where(pair_match, occupied_energy[None, None, :], 0.0), axis=(1, 2))
    own_virtual = lax.dynamic_slice_in_dim(virtual_energy, qstart, quarter, 0)
    own = (integrals, row_energy)
    window = [own]
    current = passed_along((own[0], own[1]), "blk", -(HOPS - HOPS // 2))
    window = [current]
    for turn in range(HOPS):
        current = step_down(current)
        window.append(current)
    factors = lax.all_to_all(amplitudes, "vb", split_axis=2, concat_axis=1, tiled=True)

    def pair_columns(inputs):
        factor, energy = inputs
        total = jnp.zeros((width, quarter), jnp.float32)
        for block, energies in window:
            denom = energies[:, None] + own_virtual[None, :] - energy
            weighted = jnp.dot(
                block, factor, precision=lax.Precision.HIGHEST, preferred_element_type=jnp.float32
            )
            total = total + jnp.dot(
                block.T,
                weighted / denom,
                precision=lax.Precision.HIGHEST,
                preferred_element_type=jnp.float32,
            )
        return total

    totals = lax.map(pair_columns, (factors, pair_energy))
    return lax.all_to_all(totals, "vb", split_axis=1, concat_axis=2, tiled=True)


def solution(mesh):
    return jax.shard_map(
        local,
        mesh=mesh,
        in_specs=(P("blk", "vb", None), P("blk", None), P("blk"), P("blk", None), P(), P()),
        out_specs=P("blk", "vb", None),
        check_vma=False,
    )
```

profile of v0, /device:TPU:0, one launch (start us, length us, event | category | flops | bytes accessed | tf_op | source)
XLA Modules:
  0.0 425.2 jit_solution(7205439664500854542)
XLA Ops:
  0.0 3.5 collective-permute-start
  3.5 22.9 %collective-permute-done = f32[256,1024]{1,0:T(8,128)S(1)} collective-permute-done((f32[256,1024]{1,0:T(8,128)}, f32[256,1024]{1,0:T(8,128)S(1)}, u32[]{:S(2)}, u32[]{:S(2)}) %collective-permute-start) | collective-permute-done | bytes 1048608 | tf_op jit(solution)/shard_map/ppermute | solution.py:12
  26.4 12.8 %collective-permute-start.2 = (f32[256,1024]{1,0:T(8,128)S(1)}, f32[256,1024]{1,0:T(8,128)S(1)}, u32[]{:S(2)}, u32[]{:S(2)}) collective-permute-start(f32[256,1024]{1,0:T(8,128)S(1)} %collective-permute-done), channel_id=1, source_target_pairs={{28,0},{0,4},{4,8},{8,12},{12,16},{16,20},{20,24},{24,28},{29,1},{... | collective-permute-start | bytes 3145736 | tf_op jit(solution)/shard_map/ppermute | solution.py:12
  39.2 15.6 %collective-permute-done.2 = f32[256,1024]{1,0:T(8,128)S(1)} collective-permute-done((f32[256,1024]{1,0:T(8,128)S(1)}, f32[256,1024]{1,0:T(8,128)S(1)}, u32[]{:S(2)}, u32[]{:S(2)}) %collective-permute-start.2) | collective-permute-done | bytes 1048608 | tf_op jit(solution)/shard_map/ppermute | solution.py:12
  54.8 5.3 %copy.15 = f32[4,256,1024]{1,0,2:T(4,128)} copy(f32[4,256,1024]{2,1,0:T(8,128)} %param.8) | data formatting | bytes 8388608 | tf_op args[0]
  60.1 5.0 %all-to-all-start = ((f32[4,256,1024]{1,0,2:T(4,128)}), f32[4,256,1024]{1,0,2:T(4,128)}, u32[]{:S(2)}, u32[]{:S(2)}) async-start(f32[4,256,1024]{1,0,2:T(4,128)} %copy.15), calls=%async_computation | async-start | bytes 8388608 | tf_op jit(solution)/shard_map/all_to_all | solution.py:39
  65.1 5.7 %collective-permute-done.4 = f32[256,1024]{1,0:T(8,128)S(1)} collective-permute-done((f32[256,1024]{1,0:T(8,128)S(1)}, f32[256,1024]{1,0:T(8,128)S(1)}, u32[]{:S(2)}, u32[]{:S(2)}) %collective-permute-start.4) | collective-permute-done | bytes 1048608 | tf_op jit(solution)/shard_map/ppermute | solution.py:12
  70.8 16.0 %collective-permute-done.6 = f32[256,1024]{1,0:T(8,128)S(1)} collective-permute-done((f32[256,1024]{1,0:T(8,128)S(1)}, f32[256,1024]{1,0:T(8,128)S(1)}, u32[]{:S(2)}, u32[]{:S(2)}) %collective-permute-start.6) | collective-permute-done | bytes 1048608 | tf_op jit(solution)/shard_map/ppermute | solution.py:12
  86.8 1.1 copy-done.1
  87.9 16.1 %collective-permute-done.8 = f32[256,1024]{1,0:T(8,128)} collective-permute-done((f32[256,1024]{1,0:T(8,128)S(1)}, f32[256,1024]{1,0:T(8,128)}, u32[]{:S(2)}, u32[]{:S(2)}) %collective-permute-start.8) | collective-permute-done | bytes 1048608 | tf_op jit(solution)/shard_map/ppermute | solution.py:12
  104.4 3.0 collective-permute-done.1
  107.4 3.0 collective-permute-start.3
  110.3 10.6 %collective-permute-done.3 = f32[256]{0:T(256)S(1)} collective-permute-done((f32[256]{0:T(256)S(1)}, f32[256]{0:T(256)S(1)}, u32[]{:S(2)}, u32[]{:S(2)}) %collective-permute-start.3) | collective-permute-done | bytes 1056 | tf_op jit(solution)/shard_map/ppermute | solution.py:12
  120.9 4.8 %collective-permute-done.5 = f32[256]{0:T(256)S(1)} collective-permute-done((f32[256]{0:T(256)S(1)}, f32[256]{0:T(256)S(1)}, u32[]{:S(2)}, u32[]{:S(2)}) %collective-permute-start.5) | collective-permute-done | bytes 1056 | tf_op jit(solution)/shard_map/ppermute | solution.py:12
  125.7 4.8 %collective-permute-done.7 = f32[256]{0:T(256)S(1)} collective-permute-done((f32[256]{0:T(256)S(1)}, f32[256]{0:T(256)S(1)}, u32[]{:S(2)}, u32[]{:S(2)}) %collective-permute-start.7) | collective-permute-done | bytes 1056 | tf_op jit(solution)/shard_map/ppermute | solution.py:12
  130.5 4.8 %collective-permute-done.9 = f32[256]{0:T(256)S(1)} collective-permute-done((f32[256]{0:T(256)S(1)}, f32[256]{0:T(256)S(1)}, u32[]{:S(2)}, u32[]{:S(2)}) %collective-permute-start.9) | collective-permute-done | bytes 1056 | tf_op jit(solution)/shard_map/ppermute | solution.py:12
  135.6 5.2 %copy.16 = f32[4,4,256,256]{3,2,1,0:T(8,128)} copy(f32[4,4,256,256]{2,0,3,1:T(4,128)} %bitcast.11) | data formatting | bytes 8388608 | tf_op jit(solution)/shard_map/all_to_all | solution.py:39
  140.8 225.5 %while.10 = (s32[]{:T(128)}, f32[4,1024,256]{2,0,1:T(4,128)}, f32[4,1024,256]{2,1,0:T(8,128)}, f32[256,1024]{1,0:T(8,128)S(1)}, f32[256]{0:T(256)S(1)}, /*index=...) while((s32[]{:T(128)}, f32[4,1024,256]{2,0,1:T(4,128)}, ...), condition=%wide.region_3.4_spmd, body=%wide.region_2.3_spmd.sunk | while | flops 9666166784 | bytes 58733852 | solution.py:57
  141.7 4.1 fusion.100
  146.8 2.5 fusion.102
  149.4 1.0 convolution_add_fusion.9
  150.4 2.5 fusion.103
  154.0 2.5 fusion.104
  157.5 3.7 fusion.105
  161.3 2.3 convolution_add_fusion.12
  163.5 3.7 fusion.106
  167.3 3.2 fusion.107
  170.5 3.6 copy.24
  174.1 23.2 %dynamic_update_slice.5 = f32[4,1024,256]{2,0,1:T(4,128)} dynamic-update-slice(f32[4,1024,256]{2,0,1:T(4,128)} %get-tuple-element.250, f32[1,1024,256]{2,0,1:T(1,128)} %copy.24, s32[]{:T(128)} %get-tuple-element.249, s32[]{:T(128)} %constant.3.clone.1..sunk, s32[]{:T(128)} %constant.3.clone.1..sunk) | dynamic-update-slice | bytes 2097156 | tf_op jit(solution)/shard_map/while/body/jit(dynamic_update_index_in_dim)/dynamic_update_slice | solution.py:57
  198.0 4.1 fusion.100
  203.2 2.5 fusion.102
  206.7 2.5 fusion.103
  210.3 2.5 fusion.104
  213.9 3.7 fusion.105
  217.6 2.3 convolution_add_fusion.12
  219.9 3.7 fusion.106
  223.6 3.2 fusion.107
  226.8 3.6 copy.24
  230.5 23.2 %dynamic_update_slice.5 = f32[4,1024,256]{2,0,1:T(4,128)} dynamic-update-slice(f32[4,1024,256]{2,0,1:T(4,128)} %get-tuple-element.250, f32[1,1024,256]{2,0,1:T(1,128)} %copy.24, s32[]{:T(128)} %get-tuple-element.249, s32[]{:T(128)} %constant.3.clone.1..sunk, s32[]{:T(128)} %constant.3.clone.1..sunk) | dynamic-update-slice | bytes 2097156 | tf_op jit(solution)/shard_map/while/body/jit(dynamic_update_index_in_dim)/dynamic_update_slice | solution.py:57
  254.4 4.1 fusion.100
  259.5 2.5 fusion.102
  262.0 1.0 convolution_add_fusion.9
  263.1 2.5 fusion.103
  266.6 2.5 fusion.104
  270.2 3.7 fusion.105
  273.9 2.3 convolution_add_fusion.12
  276.2 3.7 fusion.106
  279.9 3.2 fusion.107
  283.2 3.6 copy.24
  286.8 23.2 %dynamic_update_slice.5 = f32[4,1024,256]{2,0,1:T(4,128)} dynamic-update-slice(f32[4,1024,256]{2,0,1:T(4,128)} %get-tuple-element.250, f32[1,1024,256]{2,0,1:T(1,128)} %copy.24, s32[]{:T(128)} %get-tuple-element.249, s32[]{:T(128)} %constant.3.clone.1..sunk, s32[]{:T(128)} %constant.3.clone.1..sunk) | dynamic-update-slice | bytes 2097156 | tf_op jit(solution)/shard_map/while/body/jit(dynamic_update_index_in_dim)/dynamic_update_slice | solution.py:57
  310.7 4.1 fusion.100
  315.8 2.5 fusion.102
  318.4 1.0 convolution_add_fusion.9
  319.4 2.5 fusion.103
  323.0 2.5 fusion.104
  326.5 3.7 fusion.105
  330.3 2.3 convolution_add_fusion.12
  332.5 3.7 fusion.106
  336.3 3.2 fusion.107
  339.5 3.6 copy.24
  343.1 23.2 %dynamic_update_slice.5 = f32[4,1024,256]{2,0,1:T(4,128)} dynamic-update-slice(f32[4,1024,256]{2,0,1:T(4,128)} %get-tuple-element.250, f32[1,1024,256]{2,0,1:T(1,128)} %copy.24, s32[]{:T(128)} %get-tuple-element.249, s32[]{:T(128)} %constant.3.clone.1..sunk, s32[]{:T(128)} %constant.3.clone.1..sunk) | dynamic-update-slice | bytes 2097156 | tf_op jit(solution)/shard_map/while/body/jit(dynamic_update_index_in_dim)/dynamic_update_slice | solution.py:57
  366.4 48.4 %all_to_all.36 = f32[4,1024,256]{2,0,1:T(4,128)S(1)} all-to-all(f32[4,1024,256]{2,0,1:T(4,128)} %get-tuple-element.92), channel_id=1, replica_groups=mesh['blk'=8,'vb'=4] {'vb'}, dimensions={1} | all-to-all | bytes 8388608 | tf_op jit(solution)/shard_map/all_to_all | solution.py:58
  414.8 4.7 %copy.18 = f32[4,256,4,256]{3,2,1,0:T(4,128)} copy(f32[4,256,4,256]{3,0,1,2:T(4,128)S(1)} %bitcast.132) | data formatting | bytes 8388608 | tf_op jit(solution)/shard_map/all_to_all | solution.py:58
  419.5 5.8 %all_to_all.33 = f32[4,256,1024]{2,1,0:T(8,128)} reshape(f32[4,256,4,256]{3,2,1,0:T(4,128)} %copy.18) | data formatting | bytes 8388608 | tf_op jit(solution)/shard_map/all_to_all | solution.py:58
  (58 shorter events, 16.7 us)
Async XLA Ops:
  0.0 26.4 %collective-permute-start = (f32[256,1024]{1,0:T(8,128)}, f32[256,1024]{1,0:T(8,128)S(1)}, u32[]{:S(2)}, u32[]{:S(2)}) collective-permute-start(f32[256,1024]{1,0:T(8,128)} %param.9), channel_id=1, source_target_pairs={{12,0},{16,4},{20,8},{24,12},{28,16},{0,20},{4,24},{8,28},{13,1},{... | collective-permute-start | bytes 3145736 | tf_op jit(solution)/shard_map/ppermute | solution.py:12
  26.4 28.4 %collective-permute-start.2 = (f32[256,1024]{1,0:T(8,128)S(1)}, f32[256,1024]{1,0:T(8,128)S(1)}, u32[]{:S(2)}, u32[]{:S(2)}) collective-permute-start(f32[256,1024]{1,0:T(8,128)S(1)} %collective-permute-done), channel_id=1, source_target_pairs={{28,0},{0,4},{4,8},{8,12},{12,16},{16,20},{20,24},{24,28},{29,1},{... | collective-permute-start | bytes 3145736 | tf_op jit(solution)/shard_map/ppermute | solution.py:12
  54.8 16.0 %collective-permute-start.4 = (f32[256,1024]{1,0:T(8,128)S(1)}, f32[256,1024]{1,0:T(8,128)S(1)}, u32[]{:S(2)}, u32[]{:S(2)}) collective-permute-start(f32[256,1024]{1,0:T(8,128)S(1)} %collective-permute-done.2), channel_id=1, source_target_pairs={{28,0},{0,4},{4,8},{8,12},{12,16},{16,20},{20,24},{24,28},{29,1},{... | collective-permute-start | bytes 3145736 | tf_op jit(solution)/shard_map/ppermute | solution.py:12
  60.1 44.0 %copy-start.3 = (f32[1024]{0:T(1024)S(1)}, f32[1024]{0:T(1024)}, u32[]{:S(2)}) copy-start(f32[1024]{0:T(1024)} %param.13) | copy-start | bytes 12292
  60.1 44.0 %copy-start.6 = (s32[256]{0:T(256)S(1)}, s32[256]{0:T(256)}, u32[]{:S(2)}) copy-start(s32[256]{0:T(256)} %param.10) | copy-start | bytes 3076
  60.1 75.2 %copy-start.4 = (f32[256]{0:T(256)S(1)}, f32[256]{0:T(256)}, u32[]{:S(2)}) copy-start(f32[256]{0:T(256)} %param.12) | copy-start | bytes 3076
  60.1 75.2 %copy-start.5 = (s32[4,2]{0,1:T(2,128)S(1)}, s32[4,2]{0,1:T(2,128)}, u32[]{:S(2)}) copy-start(s32[4,2]{0,1:T(2,128)} %param.11) | copy-start | bytes 100
  60.1 75.5 %all-to-all-start = ((f32[4,256,1024]{1,0,2:T(4,128)}), f32[4,256,1024]{1,0,2:T(4,128)}, u32[]{:S(2)}, u32[]{:S(2)}) async-start(f32[4,256,1024]{1,0,2:T(4,128)} %copy.15), calls=%async_computation | async-start | bytes 8388608 | tf_op jit(solution)/shard_map/all_to_all | solution.py:39
  70.8 16.0 %collective-permute-start.6 = (f32[256,1024]{1,0:T(8,128)S(1)}, f32[256,1024]{1,0:T(8,128)S(1)}, u32[]{:S(2)}, u32[]{:S(2)}) collective-permute-start(f32[256,1024]{1,0:T(8,128)S(1)} %collective-permute-done.4), channel_id=1, source_target_pairs={{28,0},{0,4},{4,8},{8,12},{12,16},{16,20},{20,24},{24,28},{29,1},{... | collective-permute-start | bytes 3145736 | tf_op jit(solution)/shard_map/ppermute | solution.py:12
  86.8 1.1 copy-start.1
  87.9 16.1 %collective-permute-start.8 = (f32[256,1024]{1,0:T(8,128)S(1)}, f32[256,1024]{1,0:T(8,128)}, u32[]{:S(2)}, u32[]{:S(2)}) collective-permute-start(f32[256,1024]{1,0:T(8,128)S(1)} %collective-permute-done.6), channel_id=1, source_target_pairs={{28,0},{0,4},{4,8},{8,12},{12,16},{16,20},{20,24},{24,28},{29,1},{... | collective-permute-start | bytes 3145736 | tf_op jit(solution)/shard_map/ppermute | solution.py:12
  104.0 36.8 %collective-permute-start.10 = (f32[256,1024]{1,0:T(8,128)}, f32[256,1024]{1,0:T(8,128)}, u32[]{:S(2)}, u32[]{:S(2)}) collective-permute-start(f32[256,1024]{1,0:T(8,128)} %collective-permute-done.8), channel_id=1, source_target_pairs={{28,0},{0,4},{4,8},{8,12},{12,16},{16,20},{20,24},{24,28},{29,1},{... | collective-permute-start | bytes 3145736 | tf_op jit(solution)/shard_map/ppermute | solution.py:12
  104.3 3.1 collective-permute-start.1
  107.4 13.5 %collective-permute-start.3 = (f32[256]{0:T(256)S(1)}, f32[256]{0:T(256)S(1)}, u32[]{:S(2)}, u32[]{:S(2)}) collective-permute-start(f32[256]{0:T(256)S(1)} %collective-permute-done.1), channel_id=1, source_target_pairs={{28,0},{0,4},{4,8},{8,12},{12,16},{16,20},{20,24},{24,28},{29,1},{... | collective-permute-start | bytes 3080 | tf_op jit(solution)/shard_map/ppermute | solution.py:12
  120.9 4.8 %collective-permute-start.5 = (f32[256]{0:T(256)S(1)}, f32[256]{0:T(256)S(1)}, u32[]{:S(2)}, u32[]{:S(2)}) collective-permute-start(f32[256]{0:T(256)S(1)} %collective-permute-done.3), channel_id=1, source_target_pairs={{28,0},{0,4},{4,8},{8,12},{12,16},{16,20},{20,24},{24,28},{29,1},{... | collective-permute-start | bytes 3080 | tf_op jit(solution)/shard_map/ppermute | solution.py:12
  125.7 4.8 %collective-permute-start.7 = (f32[256]{0:T(256)S(1)}, f32[256]{0:T(256)S(1)}, u32[]{:S(2)}, u32[]{:S(2)}) collective-permute-start(f32[256]{0:T(256)S(1)} %collective-permute-done.5), channel_id=1, source_target_pairs={{28,0},{0,4},{4,8},{8,12},{12,16},{16,20},{20,24},{24,28},{29,1},{... | collective-permute-start | bytes 3080 | tf_op jit(solution)/shard_map/ppermute | solution.py:12
  130.5 4.8 %collective-permute-start.9 = (f32[256]{0:T(256)S(1)}, f32[256]{0:T(256)S(1)}, u32[]{:S(2)}, u32[]{:S(2)}) collective-permute-start(f32[256]{0:T(256)S(1)} %collective-permute-done.7), channel_id=1, source_target_pairs={{28,0},{0,4},{4,8},{8,12},{12,16},{16,20},{20,24},{24,28},{29,1},{... | collective-permute-start | bytes 3080 | tf_op jit(solution)/shard_map/ppermute | solution.py:12
  135.3 5.5 %collective-permute-start.11 = (f32[256]{0:T(256)S(1)}, f32[256]{0:T(256)S(1)}, u32[]{:S(2)}, u32[]{:S(2)}) collective-permute-start(f32[256]{0:T(256)S(1)} %collective-permute-done.9), channel_id=1, source_target_pairs={{28,0},{0,4},{4,8},{8,12},{12,16},{16,20},{20,24},{24,28},{29,1},{... | collective-permute-start | bytes 3080 | tf_op jit(solution)/shard_map/ppermute | solution.py:12
  141.0 5.8 %copy-start = (f32[4,1024,256]{2,1,0:T(8,128)S(1)}, f32[4,1024,256]{2,1,0:T(8,128)}, u32[]{:S(2)}) copy-start(f32[4,1024,256]{2,1,0:T(8,128)} %get-tuple-element.270) | copy-start | bytes 12582916 | tf_op jit(solution)/shard_map/while
  149.3 4.6 %copy-start.2 = (f32[256,1024]{1,0:T(8,128)S(1)}, f32[256,1024]{1,0:T(8,128)}, u32[]{:S(2)}) copy-start(f32[256,1024]{1,0:T(8,128)} %get-tuple-element.279) | copy-start | bytes 3145732 | tf_op jit(solution)/shard_map/while
  197.4 5.8 %copy-start = (f32[4,1024,256]{2,1,0:T(8,128)S(1)}, f32[4,1024,256]{2,1,0:T(8,128)}, u32[]{:S(2)}) copy-start(f32[4,1024,256]{2,1,0:T(8,128)} %get-tuple-element.270) | copy-start | bytes 12582916 | tf_op jit(solution)/shard_map/while
  205.7 4.6 %copy-start.2 = (f32[256,1024]{1,0:T(8,128)S(1)}, f32[256,1024]{1,0:T(8,128)}, u32[]{:S(2)}) copy-start(f32[256,1024]{1,0:T(8,128)} %get-tuple-element.279) | copy-start | bytes 3145732 | tf_op jit(solution)/shard_map/while
  253.7 5.8 %copy-start = (f32[4,1024,256]{2,1,0:T(8,128)S(1)}, f32[4,1024,256]{2,1,0:T(8,128)}, u32[]{:S(2)}) copy-start(f32[4,1024,256]{2,1,0:T(8,128)} %get-tuple-element.270) | copy-start | bytes 12582916 | tf_op jit(solution)/shard_map/while
  262.0 4.6 %copy-start.2 = (f32[256,1024]{1,0:T(8,128)S(1)}, f32[256,1024]{1,0:T(8,128)}, u32[]{:S(2)}) copy-start(f32[256,1024]{1,0:T(8,128)} %get-tuple-element.279) | copy-start | bytes 3145732 | tf_op jit(solution)/shard_map/while
  310.1 5.8 %copy-start = (f32[4,1024,256]{2,1,0:T(8,128)S(1)}, f32[4,1024,256]{2,1,0:T(8,128)}, u32[]{:S(2)}) copy-start(f32[4,1024,256]{2,1,0:T(8,128)} %get-tuple-element.270) | copy-start | bytes 12582916 | tf_op jit(solution)/shard_map/while
  318.4 4.6 %copy-start.2 = (f32[256,1024]{1,0:T(8,128)S(1)}, f32[256,1024]{1,0:T(8,128)}, u32[]{:S(2)}) copy-start(f32[256,1024]{1,0:T(8,128)} %get-tuple-element.279) | copy-start | bytes 3145732 | tf_op jit(solution)/shard_map/while
where the time goes:
time: 429 us; the launch traced here: 425 us
  local copies, waits for them, and re-layouts  132 us (31%)
  matrix products  115 us (27%)
  waiting for transfers between devices  104 us (24%)
  blocking collectives  48.4 us (11%)
  starting transfers between devices  24.3 us (6%)
    dynamic_update_slice x8, local copies, waits for them, and re-layouts, local(): totals = lax.map(pair_columns, (factors, pair_energy))  107 us
    ppermute x12, waiting for transfers between devices, passed_along(): return lax.ppermute(block, axis, route)  104 us
    dot_general x24, matrix products, pair_columns(): jnp.dot(block, factor, precision=lax.Precision.HIGHEST, preferred_element...  76.2 us
    all_to_all x1, blocking collectives, local(): return lax.all_to_all(totals, 'vb', split_axis=1, concat_axis=2, tiled=True)  48.4 us
    dot_general x24, matrix products, pair_columns(): jnp.dot(block.T, weighted / denom, precision=lax.Precision.HIGHEST, prefe...  38.5 us
    ppermute x12, starting transfers between devices, passed_along(): return lax.ppermute(block, axis, route)  19.3 us
    all_to_all x2, local copies, waits for them, and re-layouts, local(): return lax.all_to_all(totals, 'vb', split_axis=1, concat_axis=2, tiled=True)  10.4 us
  transfers between devices with their start and end apart: 13, of which 10 were waited for; matrix products, arithmetic and copies ran while one was open for 3% of the time, Pallas kernels for 0%

commit v1 on v0

--- a/solution.py
+++ b/solution.py
@@ -1,9 +1,41 @@
+import functools
 import jax
 import jax.numpy as jnp
 from jax import lax
 from jax.sharding import PartitionSpec as P
 
 HOPS = 5
+
+
+def drive_quarters_here(mine_x, join_dim, arr):
+    placed, small = (mine_x.shape[:join_dim], mine_x.shape[join_dim + 1 :])
+    return jnp.moveaxis(mine_x.reshape(*placed, arr, -1, *small), join_dim, 0)
+
+
+def map_modes(load, k_dim):
+    load = jnp.moveaxis(load, 0, k_dim)
+    current_value = load.shape
+    return load.reshape(
+        *current_value[:k_dim],
+        current_value[k_dim] * current_value[k_dim + 1],
+        *current_value[k_dim + 2 :]
+    )
+
+
+def register_widths(x_part, mesh_ax, xin, array_in):
+    moved, z_new = (lax.psum(1, axis_name=mesh_ax), lax.axis_index(mesh_ax))
+    u1 = drive_quarters_here(x_part, xin, moved)
+    rack = [u1[z_new]]
+    for h in tuple(range(1, moved)):
+        base_arr = u1[z_new ^ h]
+        rack.append(
+            lax.ppermute(base_arr, axis_name=mesh_ax, perm=[(num, num ^ h) for num in range(moved)])
+        )
+    u1 = jnp.stack(rack)[z_new ^ jnp.arange(moved)]
+    return map_modes(u1, array_in)
+
+
+knots_connect = functools.partial(register_widths, mesh_ax="vb", xin=2, array_in=1)
 
 
 def passed_along(block, axis, distance):
@@ -36,7 +68,7 @@
     for turn in range(HOPS):
         current = step_down(current)
         window.append(current)
-    factors = lax.all_to_all(amplitudes, "vb", split_axis=2, concat_axis=1, tiled=True)
+    factors = knots_connect(amplitudes)
 
     def pair_columns(inputs):
         factor, energy = inputs

time: 429 us -> 461 us (1.075)
  local copies, waits for them, and re-layouts: 132 us -> 153 us
  matrix products: 115 us -> 123 us
    another operation x0 -> x1, local copies, waits for them, and re-layouts: none -> 11.5 us
    ppermute x12, waiting for transfers between devices: 104 us -> 94.2 us  [passed_along(): return lax.ppermute(block, axis, route)]
    ppermute x0 -> x3, waiting for transfers between devices: none -> 9.3 us  [register_widths(): lax.ppermute(base_arr, axis_name=mesh_ax, perm=[(num, num ^ h) for num in...]
    reshape x0 -> x1, local copies, waits for them, and re-layouts: none -> 5.61 us  [drive_quarters_here(): return jnp.moveaxis(mine_x.reshape(*placed, arr, -1, *small), join_dim, 0)]
    all_to_all x1 -> x0, local copies, waits for them, and re-layouts: 5.25 us -> none  [local(): lax.all_to_all(amplitudes, 'vb', split_axis=2, concat_axis=1, tiled=True)]
    all_to_all x1 -> x0, starting transfers between devices: 5 us -> none  [local(): lax.all_to_all(amplitudes, 'vb', split_axis=2, concat_axis=1, tiled=True)]
    gather x0 -> x1, local copies, waits for them, and re-layouts: none -> 4.98 us  [register_widths(): u1 = jnp.stack(rack)[z_new ^ jnp.arange(moved)]]
    dot_general x24, matrix products: 38.5 us -> 43.4 us  [pair_columns(): jnp.dot(block.T, weighted / denom, precision=lax.Precision.HIGHEST, prefe...]
  transfers between devices with their start and end apart: 13 -> 15, of which waited for: 10 -> 10; matrix products, arithmetic and copies ran while one was open for 3% -> 8% of each run, Pallas kernels for 0% -> 0%
where the time goes in v1:
time: 461 us; the launch traced here: 455 us
  local copies, waits for them, and re-layouts  153 us (33%)
  matrix products  123 us (27%)
  waiting for transfers between devices  103 us (22%)
  blocking collectives  45.9 us (10%)
  starting transfers between devices  24.6 us (5%)
  other arithmetic  4.98 us (1%)
    dynamic_update_slice x8, local copies, waits for them, and re-layouts, local(): totals = lax.map(pair_columns, (factors, pair_energy))  107 us
    ppermute x12, waiting for transfers between devices, passed_along(): return lax.ppermute(block, axis, route)  94.2 us
    dot_general x24, matrix products, pair_columns(): jnp.dot(block, factor, precision=lax.Precision.HIGHEST, preferred_element...  79.6 us
    all_to_all x1, blocking collectives, local(): return lax.all_to_all(totals, 'vb', split_axis=1, concat_axis=2, tiled=True)  45.9 us
    dot_general x24, matrix products, pair_columns(): jnp.dot(block.T, weighted / denom, precision=lax.Precision.HIGHEST, prefe...  43.4 us
    ppermute x12, starting transfers between devices, passed_along(): return lax.ppermute(block, axis, route)  21.2 us
    another operation x1, local copies, waits for them, and re-layouts  11.5 us
    all_to_all x2, local copies, waits for them, and re-layouts, local(): return lax.all_to_all(totals, 'vb', split_axis=1, concat_axis=2, tiled=True)  10.4 us
  transfers between devices with their start and end apart: 15, of which 10 were waited for; matrix products, arithmetic and copies ran while one was open for 8% of the time, Pallas kernels for 0%

profile of v1, /device:TPU:0, one launch (start us, length us, event | category | flops | bytes accessed | tf_op | source)
XLA Modules:
  0.0 455.1 jit_solution(4471318071650318851)
XLA Ops:
  0.0 3.5 collective-permute-start.3
  3.5 22.9 %collective-permute-done.3 = f32[256,1024]{1,0:T(8,128)S(1)} collective-permute-done((f32[256,1024]{1,0:T(8,128)}, f32[256,1024]{1,0:T(8,128)S(1)}, u32[]{:S(2)}, u32[]{:S(2)}) %collective-permute-start.3) | collective-permute-done | bytes 1048608 | tf_op jit(solution)/shard_map/ppermute | solution.py:44
  26.4 12.8 %collective-permute-start.5 = (f32[256,1024]{1,0:T(8,128)S(1)}, f32[256,1024]{1,0:T(8,128)S(1)}, u32[]{:S(2)}, u32[]{:S(2)}) collective-permute-start(f32[256,1024]{1,0:T(8,128)S(1)} %collective-permute-done.3), channel_id=1, source_target_pairs={{28,0},{0,4},{4,8},{8,12},{12,16},{16,20},{20,24},{24,28},{29,1},{... | collective-permute-start | bytes 3145736 | tf_op jit(solution)/shard_map/ppermute | solution.py:44
  39.2 15.6 %collective-permute-done.5 = f32[256,1024]{1,0:T(8,128)S(1)} collective-permute-done((f32[256,1024]{1,0:T(8,128)S(1)}, f32[256,1024]{1,0:T(8,128)S(1)}, u32[]{:S(2)}, u32[]{:S(2)}) %collective-permute-start.5) | collective-permute-done | bytes 1048608 | tf_op jit(solution)/shard_map/ppermute | solution.py:44
  54.8 16.0 %collective-permute-done.7 = f32[256,1024]{1,0:T(8,128)S(1)} collective-permute-done((f32[256,1024]{1,0:T(8,128)S(1)}, f32[256,1024]{1,0:T(8,128)S(1)}, u32[]{:S(2)}, u32[]{:S(2)}) %collective-permute-start.7) | collective-permute-done | bytes 1048608 | tf_op jit(solution)/shard_map/ppermute | solution.py:44
  70.8 16.1 %collective-permute-done.9 = f32[256,1024]{1,0:T(8,128)} collective-permute-done((f32[256,1024]{1,0:T(8,128)S(1)}, f32[256,1024]{1,0:T(8,128)}, u32[]{:S(2)}, u32[]{:S(2)}) %collective-permute-start.9) | collective-permute-done | bytes 1048608 | tf_op jit(solution)/shard_map/ppermute | solution.py:44
  86.9 5.6 %reshape.40 = f32[4,256,4,256]{3,2,1,0:T(4,128)} reshape(f32[4,256,1024]{2,1,0:T(8,128)} %param.8) | data formatting | bytes 8388608 | tf_op jit(solution)/shard_map/reshape | solution.py:12
  92.6 11.5 %constant_dynamic-slice_fusion.3 = (f32[4,256,1,256]{3,2,1,0:T(1,128)}, f32[4,256,1,256]{3,2,1,0:T(1,128)S(1)}, f32[4,256,1,256]{3,2,1,0:T(1,128)S(1)}, f32[4,256,1,256]{3,2,1,0:T(1,128)S(1)}) fusion(f32[4,256,4,256]{3,2,1,0:T(4,128)} %reshape.40, s32[]{:T(128)S(6)} %select_n.33, s32[]{:T(128)S(6)} %select_n.35, s32[]{:T(128)S(6)} %select_n.34, s32[]{:T(128)S(6)} %select_n.36), kind=kLoop, calls=%fused_computation.51 | loop fusion | bytes 8388624 | tf_op jit(solution)/shard_map/dynamic-slice
  111.0 3.0 collective-permute-done.4
  114.0 4.8 %collective-permute-start.6 = (f32[256]{0:T(256)S(1)}, f32[256]{0:T(256)S(1)}, u32[]{:S(2)}, u32[]{:S(2)}) collective-permute-start(f32[256]{0:T(256)S(1)} %collective-permute-done.4), channel_id=1, source_target_pairs={{28,0},{0,4},{4,8},{8,12},{12,16},{16,20},{20,24},{24,28},{29,1},{... | collective-permute-start | bytes 3080 | tf_op jit(solution)/shard_map/ppermute | solution.py:44
  118.8 8.8 %collective-permute-done.6 = f32[256]{0:T(256)S(1)} collective-permute-done((f32[256]{0:T(256)S(1)}, f32[256]{0:T(256)S(1)}, u32[]{:S(2)}, u32[]{:S(2)}) %collective-permute-start.6) | collective-permute-done | bytes 1056 | tf_op jit(solution)/shard_map/ppermute | solution.py:44
  127.8 4.6 %collective-permute-done.8 = f32[256]{0:T(256)S(1)} collective-permute-done((f32[256]{0:T(256)S(1)}, f32[256]{0:T(256)S(1)}, u32[]{:S(2)}, u32[]{:S(2)}) %collective-permute-start.8) | collective-permute-done | bytes 1056 | tf_op jit(solution)/shard_map/ppermute | solution.py:44
  132.4 4.8 %collective-permute-done.10 = f32[256]{0:T(256)S(1)} collective-permute-done((f32[256]{0:T(256)S(1)}, f32[256]{0:T(256)S(1)}, u32[]{:S(2)}, u32[]{:S(2)}) %collective-permute-start.10) | collective-permute-done | bytes 1056 | tf_op jit(solution)/shard_map/ppermute | solution.py:44
  137.2 2.3 copy.52
  139.6 2.4 collective-permute-done.12
  142.0 9.3 %collective-permute-done.1 = f32[4,256,256]{2,1,0:T(8,128)} collective-permute-done((f32[4,256,256]{2,1,0:T(8,128)}, f32[4,256,256]{2,1,0:T(8,128)}, u32[]{:S(2)}, u32[]{:S(2)}) %collective-permute-start.1) | collective-permute-done | bytes 1048608 | tf_op jit(solution)/shard_map/ppermute | solution.py:32
  151.3 4.5 pad_maximum_fusion
  155.8 5.0 %gather_fusion = f32[4,4,256,256]{3,2,1,0:T(8,128)} fusion(f32[4,4,256,256]{3,2,1,0:T(8,128)} %pad_maximum_fusion, s32[1024]{0:T(1024)S(1)} %pad_clamp_fusion), kind=kCustom, calls=%fused_computation | custom fusion | bytes 8388624 | tf_op jit(solution)/shard_map/gather | solution.py:34
  160.8 4.6 %copy.34 = f32[4,4,256,256]{3,2,1,0:T(8,128)} copy(f32[4,4,256,256]{3,2,0,1:T(8,128)} %bitcast.147) | data formatting | bytes 8388608 | tf_op jit(solution)/shard_map/transpose | solution.py:16
  165.4 233.3 %while.10 = (s32[]{:T(128)}, f32[4,1024,256]{2,0,1:T(4,128)}, f32[4,1024,256]{2,1,0:T(8,128)}, f32[256,1024]{1,0:T(8,128)S(1)}, f32[256]{0:T(256)S(1)}, /*index=...) while((s32[]{:T(128)}, f32[4,1024,256]{2,0,1:T(4,128)}, ...), condition=%wide.region_3.4_spmd, body=%wide.region_2.3_spmd.sunk | while | flops 9666166784 | bytes 54539520 | solution.py:89
  166.0 4.0 fusion.101
  171.0 2.5 fusion.103
  174.5 2.5 fusion.104
  178.0 3.7 fusion.105
  181.7 2.3 convolution_add_fusion.11
  183.9 3.7 fusion.106
  187.6 2.3 convolution_add_fusion.12
  189.9 3.7 fusion.107
  193.6 3.2 fusion.108
  196.8 3.6 copy.54
  200.4 23.2 %dynamic_update_slice.5 = f32[4,1024,256]{2,0,1:T(4,128)} dynamic-update-slice(f32[4,1024,256]{2,0,1:T(4,128)} %get-tuple-element.254, f32[1,1024,256]{2,0,1:T(1,128)} %copy.54, s32[]{:T(128)} %get-tuple-element.253, s32[]{:T(128)} %constant.3.clone.1..sunk, s32[]{:T(128)} %constant.3.clone.1..sunk) | dynamic-update-slice | bytes 2097156 | tf_op jit(solution)/shard_map/while/body/jit(dynamic_update_index_in_dim)/dynamic_update_slice | solution.py:89
  224.3 4.0 fusion.101
  229.3 2.5 fusion.103
  232.8 2.5 fusion.104
  236.3 3.7 fusion.105
  240.0 2.3 convolution_add_fusion.11
  242.3 3.7 fusion.106
  246.0 2.3 convolution_add_fusion.12
  248.2 3.7 fusion.107
  251.9 3.2 fusion.108
  255.2 3.6 copy.54
  258.8 23.2 %dynamic_update_slice.5 = f32[4,1024,256]{2,0,1:T(4,128)} dynamic-update-slice(f32[4,1024,256]{2,0,1:T(4,128)} %get-tuple-element.254, f32[1,1024,256]{2,0,1:T(1,128)} %copy.54, s32[]{:T(128)} %get-tuple-element.253, s32[]{:T(128)} %constant.3.clone.1..sunk, s32[]{:T(128)} %constant.3.clone.1..sunk) | dynamic-update-slice | bytes 2097156 | tf_op jit(solution)/shard_map/while/body/jit(dynamic_update_index_in_dim)/dynamic_update_slice | solution.py:89
  282.6 4.0 fusion.101
  287.7 2.5 fusion.103
  291.2 2.5 fusion.104
  294.7 3.7 fusion.105
  300.6 3.7 fusion.106
  306.6 3.7 fusion.107
  310.2 3.2 fusion.108
  313.5 3.6 copy.54
  317.1 23.2 %dynamic_update_slice.5 = f32[4,1024,256]{2,0,1:T(4,128)} dynamic-update-slice(f32[4,1024,256]{2,0,1:T(4,128)} %get-tuple-element.254, f32[1,1024,256]{2,0,1:T(1,128)} %copy.54, s32[]{:T(128)} %get-tuple-element.253, s32[]{:T(128)} %constant.3.clone.1..sunk, s32[]{:T(128)} %constant.3.clone.1..sunk) | dynamic-update-slice | bytes 2097156 | tf_op jit(solution)/shard_map/while/body/jit(dynamic_update_index_in_dim)/dynamic_update_slice | solution.py:89
  341.0 4.0 fusion.101
  346.0 2.5 fusion.103
  349.5 2.5 fusion.104
  353.0 3.7 fusion.105
  356.7 2.3 convolution_add_fusion.11
  358.9 3.7 fusion.106
  364.9 3.7 fusion.107
  368.6 3.2 fusion.108
  371.8 3.6 copy.54
  375.4 23.2 %dynamic_update_slice.5 = f32[4,1024,256]{2,0,1:T(4,128)} dynamic-update-slice(f32[4,1024,256]{2,0,1:T(4,128)} %get-tuple-element.254, f32[1,1024,256]{2,0,1:T(1,128)} %copy.54, s32[]{:T(128)} %get-tuple-element.253, s32[]{:T(128)} %constant.3.clone.1..sunk, s32[]{:T(128)} %constant.3.clone.1..sunk) | dynamic-update-slice | bytes 2097156 | tf_op jit(solution)/shard_map/while/body/jit(dynamic_update_index_in_dim)/dynamic_update_slice | solution.py:89
  398.7 45.9 %all_to_all.18 = f32[4,1024,256]{2,0,1:T(4,128)S(1)} all-to-all(f32[4,1024,256]{2,0,1:T(4,128)} %get-tuple-element.92), channel_id=1, replica_groups=mesh['blk'=8,'vb'=4] {'vb'}, dimensions={1} | all-to-all | bytes 8388608 | tf_op jit(solution)/shard_map/all_to_all | solution.py:90
  444.6 4.7 %copy.36 = f32[4,256,4,256]{3,2,1,0:T(4,128)} copy(f32[4,256,4,256]{3,0,1,2:T(4,128)S(1)} %bitcast.148) | data formatting | bytes 8388608 | tf_op jit(solution)/shard_map/all_to_all | solution.py:90
  449.3 5.8 %all_to_all.16 = f32[4,256,1024]{2,1,0:T(8,128)} reshape(f32[4,256,4,256]{3,2,1,0:T(4,128)} %copy.36) | data formatting | bytes 8388608 | tf_op jit(solution)/shard_map/all_to_all | solution.py:90
  (61 shorter events, 28.8 us)
Async XLA Ops:
  0.0 26.4 %collective-permute-start.3 = (f32[256,1024]{1,0:T(8,128)}, f32[256,1024]{1,0:T(8,128)S(1)}, u32[]{:S(2)}, u32[]{:S(2)}) collective-permute-start(f32[256,1024]{1,0:T(8,128)} %param.9), channel_id=1, source_target_pairs={{12,0},{16,4},{20,8},{24,12},{28,16},{0,20},{4,24},{8,28},{13,1},{... | collective-permute-start | bytes 3145736 | tf_op jit(solution)/shard_map/ppermute | solution.py:44
  26.4 28.4 %collective-permute-start.5 = (f32[256,1024]{1,0:T(8,128)S(1)}, f32[256,1024]{1,0:T(8,128)S(1)}, u32[]{:S(2)}, u32[]{:S(2)}) collective-permute-start(f32[256,1024]{1,0:T(8,128)S(1)} %collective-permute-done.3), channel_id=1, source_target_pairs={{28,0},{0,4},{4,8},{8,12},{12,16},{16,20},{20,24},{24,28},{29,1},{... | collective-permute-start | bytes 3145736 | tf_op jit(solution)/shard_map/ppermute | solution.py:44
  54.8 16.0 %collective-permute-start.7 = (f32[256,1024]{1,0:T(8,128)S(1)}, f32[256,1024]{1,0:T(8,128)S(1)}, u32[]{:S(2)}, u32[]{:S(2)}) collective-permute-start(f32[256,1024]{1,0:T(8,128)S(1)} %collective-permute-done.5), channel_id=1, source_target_pairs={{28,0},{0,4},{4,8},{8,12},{12,16},{16,20},{20,24},{24,28},{29,1},{... | collective-permute-start | bytes 3145736 | tf_op jit(solution)/shard_map/ppermute | solution.py:44
  70.8 16.1 %collective-permute-start.9 = (f32[256,1024]{1,0:T(8,128)S(1)}, f32[256,1024]{1,0:T(8,128)}, u32[]{:S(2)}, u32[]{:S(2)}) collective-permute-start(f32[256,1024]{1,0:T(8,128)S(1)} %collective-permute-done.7), channel_id=1, source_target_pairs={{28,0},{0,4},{4,8},{8,12},{12,16},{16,20},{20,24},{24,28},{29,1},{... | collective-permute-start | bytes 3145736 | tf_op jit(solution)/shard_map/ppermute | solution.py:44
  86.9 23.8 %collective-permute-start.11 = (f32[256,1024]{1,0:T(8,128)}, f32[256,1024]{1,0:T(8,128)}, u32[]{:S(2)}, u32[]{:S(2)}) collective-permute-start(f32[256,1024]{1,0:T(8,128)} %collective-permute-done.9), channel_id=1, source_target_pairs={{28,0},{0,4},{4,8},{8,12},{12,16},{16,20},{20,24},{24,28},{29,1},{... | collective-permute-start | bytes 3145736 | tf_op jit(solution)/shard_map/ppermute | solution.py:44
  104.1 6.6 %copy-start.1 = (f32[1024]{0:T(1024)S(1)}, f32[1024]{0:T(1024)}, u32[]{:S(2)}) copy-start(f32[1024]{0:T(1024)} %param.13) | copy-start | bytes 12292
  104.1 6.7 %copy-start.4 = (s32[256]{0:T(256)S(1)}, s32[256]{0:T(256)}, u32[]{:S(2)}) copy-start(s32[256]{0:T(256)} %param.10) | copy-start | bytes 3076
  104.1 23.5 %copy-start.2 = (f32[256]{0:T(256)S(1)}, f32[256]{0:T(256)}, u32[]{:S(2)}) copy-start(f32[256]{0:T(256)} %param.12) | copy-start | bytes 3076
  104.1 23.5 %copy-start.3 = (s32[4,2]{0,1:T(2,128)S(1)}, s32[4,2]{0,1:T(2,128)}, u32[]{:S(2)}) copy-start(s32[4,2]{0,1:T(2,128)} %param.11) | copy-start | bytes 100
  105.1 36.8 %collective-permute-start = (f32[4,256,256]{2,1,0:T(8,128)}, f32[4,256,256]{2,1,0:T(8,128)}, u32[]{:S(2)}, u32[]{:S(2)}) collective-permute-start(f32[4,256,256]{2,1,0:T(8,128)} %bitcast.80), channel_id=1, source_target_pairs={{0,1},{1,0},{2,3},{3,2},{4,5},{5,4},{6,7},{7,6},{8,9},{9,8},{10,11... | collective-permute-start | bytes 3145736 | tf_op jit(solution)/shard_map/ppermute | solution.py:32
  107.7 43.6 %collective-permute-start.1 = (f32[4,256,256]{2,1,0:T(8,128)}, f32[4,256,256]{2,1,0:T(8,128)}, u32[]{:S(2)}, u32[]{:S(2)}) collective-permute-start(f32[4,256,256]{2,1,0:T(8,128)} %bitcast.79), channel_id=1, source_target_pairs={{0,2},{1,3},{2,0},{3,1},{4,6},{5,7},{6,4},{7,5},{8,10},{9,11},{10,... | collective-permute-start | bytes 3145736 | tf_op jit(solution)/shard_map/ppermute | solution.py:32
  110.2 41.0 %collective-permute-start.2 = (f32[4,256,256]{2,1,0:T(8,128)}, f32[4,256,256]{2,1,0:T(8,128)}, u32[]{:S(2)}, u32[]{:S(2)}) collective-permute-start(f32[4,256,256]{2,1,0:T(8,128)} %bitcast.78), channel_id=1, source_target_pairs={{0,3},{1,2},{2,1},{3,0},{4,7},{5,6},{6,5},{7,4},{8,11},{9,10},{10,... | collective-permute-start | bytes 3145736 | tf_op jit(solution)/shard_map/ppermute | solution.py:32
  110.7 54.6 %collective-permute-start.13 = (f32[256,1024]{1,0:T(8,128)}, f32[256,1024]{1,0:T(8,128)}, u32[]{:S(2)}, u32[]{:S(2)}) collective-permute-start(f32[256,1024]{1,0:T(8,128)} %collective-permute-done.11), channel_id=1, source_target_pairs={{28,0},{0,4},{4,8},{8,12},{12,16},{16,20},{20,24},{24,28},{29,1},{... | collective-permute-start | bytes 3145736 | tf_op jit(solution)/shard_map/ppermute | solution.py:44
  111.0 3.1 collective-permute-start.4
  114.0 13.5 %collective-permute-start.6 = (f32[256]{0:T(256)S(1)}, f32[256]{0:T(256)S(1)}, u32[]{:S(2)}, u32[]{:S(2)}) collective-permute-start(f32[256]{0:T(256)S(1)} %collective-permute-done.4), channel_id=1, source_target_pairs={{28,0},{0,4},{4,8},{8,12},{12,16},{16,20},{20,24},{24,28},{29,1},{... | collective-permute-start | bytes 3080 | tf_op jit(solution)/shard_map/ppermute | solution.py:44
  127.6 4.8 %collective-permute-start.8 = (f32[256]{0:T(256)S(1)}, f32[256]{0:T(256)S(1)}, u32[]{:S(2)}, u32[]{:S(2)}) collective-permute-start(f32[256]{0:T(256)S(1)} %collective-permute-done.6), channel_id=1, source_target_pairs={{28,0},{0,4},{4,8},{8,12},{12,16},{16,20},{20,24},{24,28},{29,1},{... | collective-permute-start | bytes 3080 | tf_op jit(solution)/shard_map/ppermute | solution.py:44
  132.4 4.8 %collective-permute-start.10 = (f32[256]{0:T(256)S(1)}, f32[256]{0:T(256)S(1)}, u32[]{:S(2)}, u32[]{:S(2)}) collective-permute-start(f32[256]{0:T(256)S(1)} %collective-permute-done.8), channel_id=1, source_target_pairs={{28,0},{0,4},{4,8},{8,12},{12,16},{16,20},{20,24},{24,28},{29,1},{... | collective-permute-start | bytes 3080 | tf_op jit(solution)/shard_map/ppermute | solution.py:44
  137.2 4.8 %collective-permute-start.12 = (f32[256]{0:T(256)S(1)}, f32[256]{0:T(256)S(1)}, u32[]{:S(2)}, u32[]{:S(2)}) collective-permute-start(f32[256]{0:T(256)S(1)} %collective-permute-done.10), channel_id=1, source_target_pairs={{28,0},{0,4},{4,8},{8,12},{12,16},{16,20},{20,24},{24,28},{29,1},{... | collective-permute-start | bytes 3080 | tf_op jit(solution)/shard_map/ppermute | solution.py:44
  142.0 23.4 %collective-permute-start.14 = (f32[256]{0:T(256)S(1)}, f32[256]{0:T(256)S(1)}, u32[]{:S(2)}, u32[]{:S(2)}) collective-permute-start(f32[256]{0:T(256)S(1)} %collective-permute-done.12), channel_id=1, source_target_pairs={{28,0},{0,4},{4,8},{8,12},{12,16},{16,20},{20,24},{24,28},{29,1},{... | collective-permute-start | bytes 3080 | tf_op jit(solution)/shard_map/ppermute | solution.py:44
  165.4 5.6 %copy-start = (f32[4,1024,256]{2,1,0:T(8,128)S(1)}, f32[4,1024,256]{2,1,0:T(8,128)}, u32[]{:S(2)}) copy-start(f32[4,1024,256]{2,1,0:T(8,128)} %get-tuple-element.274) | copy-start | bytes 12582916 | tf_op jit(solution)/shard_map/while
  223.7 5.6 %copy-start = (f32[4,1024,256]{2,1,0:T(8,128)S(1)}, f32[4,1024,256]{2,1,0:T(8,128)}, u32[]{:S(2)}) copy-start(f32[4,1024,256]{2,1,0:T(8,128)} %get-tuple-element.274) | copy-start | bytes 12582916 | tf_op jit(solution)/shard_map/while
  282.0 5.6 %copy-start = (f32[4,1024,256]{2,1,0:T(8,128)S(1)}, f32[4,1024,256]{2,1,0:T(8,128)}, u32[]{:S(2)}) copy-start(f32[4,1024,256]{2,1,0:T(8,128)} %get-tuple-element.274) | copy-start | bytes 12582916 | tf_op jit(solution)/shard_map/while
  340.3 5.6 %copy-start = (f32[4,1024,256]{2,1,0:T(8,128)S(1)}, f32[4,1024,256]{2,1,0:T(8,128)}, u32[]{:S(2)}) copy-start(f32[4,1024,256]{2,1,0:T(8,128)} %get-tuple-element.274) | copy-start | bytes 12582916 | tf_op jit(solution)/shard_map/while
